TPU v7x, 512 devices: a whole 4x8x8 slice. The times are simulated.
512 devices in a mesh: dp: 8 (over y), cls: 64 (over x, z, core).
Axes of the slice: x: 4, y: 8, z: 8, core: 2. Of those that a mesh axis runs over, the one named last changes fastest.
Arguments:
- embeddings: bfloat16 [4608, 4096], P('dp'), may hold values from -128 to 128
- fold_ids: int32 [4608], P('dp'), may hold values from 0 to 4
- labels: int32 [4608], P('dp'), may hold values from 0 to 1023
- weights: bfloat16 [4096, 5120], P('dp', 'cls'), may hold values from -4 to 4
- direction: bfloat16 [4096, 5120], P('dp', 'cls'), may hold values from -0.09375 to 0.09375
Outputs:
- gradient: float32 [4096, 5120], P('dp', 'cls')
- hess_vec: float32 [4096, 5120], P('dp', 'cls')
All inputs are finite; a program needn't handle non-finite values.
Results may differ from a plain program's by a relative error of at most 0.0055.
Values may be sent and summed in bfloat16 or wider, within the bound.
No kernel may reach another device: no remote copies, remote signals or barrier semaphores. Data moves between devices by JAX's collectives and lax.ppermute only.
A program may use at most 64 MiB of HBM per device.

v0:
```python
import jax
import jax.numpy as jnp
from jax import lax
from jax.sharding import PartitionSpec as P

D = 4096
FOLDS = 5


def local(embeddings, fold_ids, labels, weights, direction):
    row_count = embeddings.shape[0]
    columns = weights.shape[1]
    per_class = columns // FOLDS
    logits = jnp.dot(
        embeddings,
        lax.all_gather(weights, "dp", axis=0, tiled=True),
        preferred_element_type=jnp.float32,
    )
    tangent = jnp.dot(
        embeddings,
        lax.all_gather(direction, "dp", axis=0, tiled=True),
        preferred_element_type=jnp.float32,
    )
    logits = logits.reshape(row_count, per_class, FOLDS)
    tangent = tangent.reshape(row_count, per_class, FOLDS)
    local_high = jnp.max(logits, axis=1)
    highest = lax.pmax(local_high, "cls")
    scaled = jnp.exp(logits - highest[:, None, :])
    summed, moment = lax.psum((jnp.sum(scaled, axis=1), jnp.sum(scaled * tangent, axis=1)), "cls")
    probability = scaled / summed[:, None, :]
    mean_tangent = moment / summed
    class_ids = lax.axis_index("cls") * per_class + jnp.arange(per_class, dtype=jnp.int32)
    onehot = (labels[:, None] == class_ids[None, :]).astype(jnp.float32)[:, :, None]
    training = (fold_ids[:, None] != jnp.arange(FOLDS, dtype=jnp.int32)[None, :]).astype(
        jnp.float32
    )[:, None, :]
    residual_rows = (
        (training * (probability - onehot)).reshape(row_count, columns).astype(jnp.bfloat16)
    )
    curvature = (
        (training * probability * (tangent - mean_tangent[:, None, :]))
        .reshape(row_count, columns)
        .astype(jnp.bfloat16)
    )
    contract = (((0,), (0,)), ((), ()))
    share = D // lax.axis_size("dp")
    full_grad, full_hvp = lax.psum(
        (
            lax.dot_general(
                embeddings, residual_rows, contract, preferred_element_type=jnp.float32
            ),
            lax.dot_general(embeddings, curvature, contract, preferred_element_type=jnp.float32),
        ),
        "dp",
    )
    offset = lax.axis_index("dp") * share
    gradient = lax.dynamic_slice_in_dim(full_grad, offset, share, 0)
    hess_vec = lax.dynamic_slice_in_dim(full_hvp, offset, share, 0)
    return (gradient, hess_vec)


def solution(mesh):
    placed = (P("dp", None), P("dp"), P("dp"), P("dp", "cls"), P("dp", "cls"))
    return jax.shard_map(
        local,
        mesh=mesh,
        in_specs=placed,
        out_specs=(P("dp", "cls"), P("dp", "cls")),
        check_vma=False,
    )
```

profile of v0, /device:TPU:2, one launch (start us, length us, event | category | flops | bytes accessed | tf_op | source)
XLA Modules:
  0.0 670.8 jit_solution(5172615857026448851)
XLA Ops:
  7.2 0.0 all-reduce.4.cloned.1.call-start
  7.2 0.7 fusion.1
  7.9 0.8 compare_convert_fusion
  8.8 0.0 copy-start
  8.8 27.7 %all_gather.6 = bf16[4096,80]{0,1:T(8,128)(2,1)S(1)} all-gather(bf16[512,80]{0,1:T(8,128)(2,1)} %param.8), channel_id=1, replica_groups=mesh['dp'=8,'cls'=64] {'dp'}, dimensions={0}, use_global_device_ids=true | all-gather | bytes 737280 | tf_op jit(solution)/shard_map/all_gather | solution.py:16
  36.5 3.9 fusion.2
  40.5 217.1 %pmax.7 = f32[576,5]{0,1:T(8,128)S(1)} all-reduce(f32[576,5]{0,1:T(8,128)S(1)} %reduce_max.9), channel_id=1, replica_groups=mesh['dp'=8,'cls'=64] {'cls'}, use_global_device_ids=true, to_apply=%region_1.0 | all-reduce | flops 2880 | bytes 23040 | tf_op jit(solution)/shard_map/pmax | solution.py:27
  257.7 0.0 copy-done
  257.7 25.8 %all_gather.7 = bf16[4096,80]{0,1:T(8,128)(2,1)S(1)} all-gather(bf16[512,80]{0,1:T(8,128)(2,1)S(1)} %copy-done), channel_id=1, replica_groups=mesh['dp'=8,'cls'=64] {'dp'}, dimensions={0}, use_global_device_ids=true | all-gather | bytes 737280 | tf_op jit(solution)/shard_map/all_gather | solution.py:21
  283.5 3.9 fusion.3
  287.4 0.1 multiply_reduce_fusion
  287.5 246.3 %all-reduce = (f32[576,5]{0,1:T(8,128)S(1)}, f32[576,5]{0,1:T(8,128)S(1)}) all-reduce(f32[576,5]{0,1:T(8,128)S(1)} %get-tuple-element.3, f32[576,5]{0,1:T(8,128)S(1)} %get-tuple-element.2), channel_id=1, replica_groups=mesh['dp'=8,'cls'=64] {'cls'}, use_global_device_ids=true, to_apply=%region_3.0 | all-reduce | flops 5760 | bytes 46080 | tf_op jit(solution)/shard_map/psum | solution.py:29
  533.9 4.5 convolution_bitcast_fusion
  538.4 4.5 convolution_bitcast_fusion.1
  542.9 0.0 all-reduce.4.cloned.1.call-update
  542.9 119.3 %all-reduce.4.cloned.1.call-done = (f32[4096,80]{0,1:T(8,128)}, f32[4096,80]{0,1:T(8,128)}) async-done(((f32[4096,80]{0,1:T(8,128)}, f32[4096,80]{0,1:T(8,128)}), (f32[4096,80]{0,1:T(8,128)}, f32[4096,80]{0,1:T(8,128)})) %all-reduce.4.cloned.1.call-update) | async-done | bytes 2621456 | tf_op jit(solution)/shard_map/psum | solution.py:47
  662.2 1.7 constant_dynamic-slice_fusion
  (15 shorter events, 0.4 us)
Async XLA Ops:
  7.2 655.0 %all-reduce.4.cloned.1.call-start = ((), (), s32[]{:S(2)}) async-start(), calls=%async_computation | async-start | bytes 5242880 | tf_op jit(solution)/shard_map/psum | solution.py:47
  8.8 248.8 %copy-start = (bf16[512,80]{0,1:T(8,128)(2,1)S(1)}, bf16[512,80]{0,1:T(8,128)(2,1)}, u32[]{:S(2)}) copy-start(bf16[512,80]{0,1:T(8,128)(2,1)} %param.9) | copy-start | bytes 245764
Sparse Core Ops, SparseCore 0:
  543.0 119.0 all-reduce.3
where the time goes:
time: 671 us
  blocking collectives  517 us (77%)
  waiting for transfers between devices  119 us (18%)
  matrix products  16.7 us (2%)
  between operations  14.2 us (2%)
    psum x1, blocking collectives, local(): lax.psum((jnp.sum(scaled, axis=1), jnp.sum(scaled * tangent, axis=1)), 'c...  246 us
    pmax x1, blocking collectives, local(): highest = lax.pmax(local_high, 'cls')  217 us
    psum x1, waiting for transfers between devices, local(): lax.psum((lax.dot_general(embeddings, residual_rows, contract, preferred_...  119 us
    all_gather x1, blocking collectives, local(): lax.all_gather(weights, 'dp', axis=0, tiled=True)  27.7 us
    all_gather x1, blocking collectives, local(): lax.all_gather(direction, 'dp', axis=0, tiled=True)  25.8 us
  transfers between devices with their start and end apart: 1, of which 1 were waited for; matrix products, arithmetic and copies ran while one was open for 0% of the time, Pallas kernels for 0%

commit v1 on v0

--- a/solution.py
+++ b/solution.py
@@ -13,7 +13,9 @@
     per_class = columns // FOLDS
     logits = jnp.dot(
         embeddings,
-        lax.all_gather(weights, "dp", axis=0, tiled=True),
+        jnp.concatenate(
+            lax.all_to_all(jnp.stack([weights] * lax.axis_size("dp")), "dp", 0, 0), axis=0
+        ),
         preferred_element_type=jnp.float32,
     )
     tangent = jnp.dot(

time: 671 us -> 663 us (0.988)
  blocking collectives: 517 us -> 501 us
  starting transfers between devices: 0.04 us -> 7.27 us
    all_gather x1 -> x0, blocking collectives: 27.7 us -> none  [local(): lax.all_gather(weights, 'dp', axis=0, tiled=True)]
    all_gather x1, blocking collectives: 25.8 us -> 37.7 us  [local(): lax.all_gather(direction, 'dp', axis=0, tiled=True)]
    all_to_all x0 -> x1, starting transfers between devices: none -> 7.23 us  [local(): lax.all_to_all(jnp.stack([weights] * lax.axis_size('dp')), 'dp', 0, 0)]
  transfers between devices with their start and end apart: 1 -> 2, of which waited for: 1 -> 1; matrix products, arithmetic and copies ran while one was open for 0% -> 1% of each run, Pallas kernels for 0% -> 0%
where the time goes in v1:
time: 663 us
  blocking collectives  501 us (76%)
  waiting for transfers between devices  119 us (18%)
  matrix products  16.8 us (3%)
  between operations  14.1 us (2%)
  starting transfers between devices  7.27 us (1%)
    psum x1, blocking collectives, local(): lax.psum((jnp.sum(scaled, axis=1), jnp.sum(scaled * tangent, axis=1)), 'c...  246 us
    pmax x1, blocking collectives, local(): highest = lax.pmax(local_high, 'cls')  217 us
    psum x1, waiting for transfers between devices, local(): lax.psum((lax.dot_general(embeddings, residual_rows, contract, preferred_...  119 us
    all_gather x1, blocking collectives, local(): lax.all_gather(direction, 'dp', axis=0, tiled=True)  37.7 us
  transfers between devices with their start and end apart: 2, of which 1 were waited for; matrix products, arithmetic and copies ran while one was open for 1% of the time, Pallas kernels for 0%

profile of v1, /device:TPU:2, one launch (start us, length us, event | category | flops | bytes accessed | tf_op | source)
XLA Modules:
  0.0 662.6 jit_solution(15208722674363858482)
XLA Ops:
  7.2 1.8 stack.2
  8.9 0.0 copy-start.1
  8.9 0.0 copy-start
  8.9 7.2 %all-to-all-start = ((bf16[8,512,80]{1,2,0:T(8,128)(2,1)}), bf16[8,512,80]{1,2,0:T(8,128)(2,1)S(1)}, u32[]{:S(2)}, u32[]{:S(2)}) async-start(bf16[8,512,80]{1,2,0:T(8,128)(2,1)} %stack.2), calls=%async_computation | async-start | bytes 1310720 | tf_op jit(solution)/shard_map/all_to_all | solution.py:17
  16.2 0.0 all-reduce.4.cloned.1.call-start
  16.2 37.7 %all_gather.3 = bf16[4096,80]{0,1:T(8,128)(2,1)S(1)} all-gather(bf16[512,80]{0,1:T(8,128)(2,1)} %param.9), channel_id=1, replica_groups=mesh['dp'=8,'cls'=64] {'dp'}, dimensions={0}, use_global_device_ids=true | all-gather | bytes 737280 | tf_op jit(solution)/shard_map/all_gather | solution.py:23
  53.9 3.9 fusion.7
  57.9 0.0 copy-done.1
  57.9 0.0 copy-done
  57.9 0.1 compare_convert_fusion
  58.0 0.0 all-to-all-done
  58.0 0.1 copy.24
  58.1 0.3 dot_general.21
  58.3 3.9 fusion.6
  62.2 217.1 %pmax.7 = f32[576,5]{0,1:T(8,128)S(1)} all-reduce(f32[576,5]{0,1:T(8,128)S(1)} %get-tuple-element.10), channel_id=1, replica_groups=mesh['dp'=8,'cls'=64] {'cls'}, use_global_device_ids=true, to_apply=%region_1.0 | all-reduce | flops 2880 | bytes 23040 | tf_op jit(solution)/shard_map/pmax | solution.py:29
  279.3 0.1 multiply_reduce_fusion
  279.4 246.2 %all-reduce = (f32[576,5]{0,1:T(8,128)S(1)}, f32[576,5]{0,1:T(8,128)S(1)}) all-reduce(f32[576,5]{0,1:T(8,128)S(1)} %get-tuple-element.3, f32[576,5]{0,1:T(8,128)S(1)} %get-tuple-element.2), channel_id=1, replica_groups=mesh['dp'=8,'cls'=64] {'cls'}, use_global_device_ids=true, to_apply=%region_3.0 | all-reduce | flops 5760 | bytes 46080 | tf_op jit(solution)/shard_map/psum | solution.py:31
  525.6 0.1 multiply_convert_fusion
  525.8 0.1 convert_element_type.31
  525.9 0.1 convert_element_type.29
  526.0 4.5 convolution_bitcast_fusion.1
  530.5 4.5 convolution_bitcast_fusion
  535.0 0.0 all-reduce.4.cloned.1.call-update
  535.0 119.1 %all-reduce.4.cloned.1.call-done = (f32[4096,80]{0,1:T(8,128)}, f32[4096,80]{0,1:T(8,128)}) async-done(((f32[4096,80]{0,1:T(8,128)}, f32[4096,80]{0,1:T(8,128)}), (f32[4096,80]{0,1:T(8,128)}, f32[4096,80]{0,1:T(8,128)})) %all-reduce.4.cloned.1.call-update) | async-done | bytes 2621456 | tf_op jit(solution)/shard_map/psum | solution.py:49
  654.1 1.7 constant_dynamic-slice_fusion
  (6 shorter events, 0.1 us)
Async XLA Ops:
  8.9 48.9 %copy-start.1 = (s32[576]{0:T(1024)S(1)}, s32[576]{0:T(1024)}, u32[]{:S(2)}) copy-start(s32[576]{0:T(1024)} %param.6) | copy-start | bytes 6916
  8.9 49.0 %copy-start = (s32[576]{0:T(1024)S(1)}, s32[576]{0:T(1024)}, u32[]{:S(2)}) copy-start(s32[576]{0:T(1024)} %param.7) | copy-start | bytes 6916
  8.9 49.0 %all-to-all-start = ((bf16[8,512,80]{1,2,0:T(8,128)(2,1)}), bf16[8,512,80]{1,2,0:T(8,128)(2,1)S(1)}, u32[]{:S(2)}, u32[]{:S(2)}) async-start(bf16[8,512,80]{1,2,0:T(8,128)(2,1)} %stack.2), calls=%async_computation | async-start | bytes 1310720 | tf_op jit(solution)/shard_map/all_to_all | solution.py:17
  16.2 637.9 %all-reduce.4.cloned.1.call-start = ((), (), s32[]{:S(2)}) async-start(), calls=%async_computation.1 | async-start | bytes 5242880 | tf_op jit(solution)/shard_map/psum | solution.py:49
Sparse Core Ops, SparseCore 0:
  535.1 118.8 all-reduce.3
